TPU v7x, 512 devices: a whole 4x4x16 slice. The times are simulated.
512 devices in a mesh: head: 4 (over x_lo, core), seq: 128 (over x_hi, z, y).
Axes of the slice: x: 4 (x_hi: 2, x_lo: 2; x = x_hi * 2 + x_lo), y: 4, z: 16, core: 2. Of those that a mesh axis runs over, the one named last changes fastest.
Arguments:
- queries: bfloat16 [32768, 32, 128], P('seq', 'head'), may hold values from -6 to 6
- normed_keys: bfloat16 [32768, 16, 128], P('seq', 'head'), may hold values from -6 to 6
- value_matrix: bfloat16 [32768, 16, 128], P('seq', 'head'), may hold values from -6 to 6
- forward_out: bfloat16 [32768, 32, 128], P('seq', 'head'), may hold values from -1.75 to 1.75
- output_gradient: bfloat16 [32768, 32, 128], P(('seq', 'head')), may hold values from -96 to 96
- row_log_total: float32 [32, 32768], P('head', 'seq'), may hold values from 6 to 8
- pair_start: int32 [32768], P('seq'), may hold values from 0 to 32256, as said below
Outputs:
- query_grad: bfloat16 [32768, 32, 128], P(('seq', 'head'))
- key_grad: bfloat16 [32768, 16, 128], P(('seq', 'head'))
- value_grad: bfloat16 [32768, 16, 128], P(('seq', 'head'))
Inputs may be any that keep to these rules, and one draw needn't show every extreme that they name: pair_start[p] is the first position of the pair that holds token p: it never falls, never exceeds p, and equals p at each pair's first token; the last pair holds the final 1024 / 2 tokens, the pair before it at most 1024 tokens, and every other pair 1024 / 8 to 1024 tokens.
All inputs are finite; a program needn't handle non-finite values.
Results may differ from a plain program's by a relative error of at most 0.0059.
Values may be sent and summed in bfloat16 or wider, within the bound.
No kernel may reach another device: no remote copies, remote signals or barrier semaphores. Data moves between devices by JAX's collectives and lax.ppermute only.
A program may use at most 64 MiB of HBM per device.

v0:
```python
import jax
import jax.numpy as jnp
from jax import lax
from jax.sharding import Mesh
from jax.sharding import PartitionSpec as P

WINDOW_LENGTH = 1024
BLOCK = 256
score_scale = 168.0 ** (-0.5)


def shifted(value, axis, by):
    size = lax.axis_size(axis)
    pairs = [(i, i + by) for i in range(size) if 0 <= i + by < size]
    return lax.ppermute(value, axis, pairs)


def band_terms(query, grad, logsum, delta, start, base, keys, values):
    tokens, group, depth = query.shape
    tiles = tokens // BLOCK
    span = WINDOW_LENGTH + BLOCK
    query_t = query.reshape(tiles, BLOCK, group, depth)
    grad_t = grad.reshape(tiles, BLOCK, group, depth)
    logsum_t = logsum.reshape(group, tiles, BLOCK).transpose(1, 0, 2)
    delta_t = delta.reshape(group, tiles, BLOCK).transpose(1, 0, 2)
    start_t = start.reshape(tiles, BLOCK)
    key_w = jnp.stack([keys[t * BLOCK : t * BLOCK + span] for t in range(tiles)])
    value_w = jnp.stack([values[t * BLOCK : t * BLOCK + span] for t in range(tiles)])
    tile_base = base + BLOCK * jnp.arange(tiles, dtype=jnp.int32)
    query_place = tile_base[:, None] + jnp.arange(BLOCK, dtype=jnp.int32)[None, :]
    key_place = tile_base[:, None] - WINDOW_LENGTH + jnp.arange(span, dtype=jnp.int32)[None, :]
    gap = query_place[:, :, None] - key_place[:, None, :]
    visible = (gap >= 0) & (gap < WINDOW_LENGTH) & (key_place[:, None, :] >= start_t[:, :, None])
    scores = (
        jnp.einsum("tigd,tjd->tgij", query_t, key_w, preferred_element_type=jnp.float32)
        * score_scale
    )
    probs = jnp.where(visible[:, None], jnp.exp(scores - logsum_t[..., None]), 0.0)
    dprobs = jnp.einsum("tigd,tjd->tgij", grad_t, value_w, preferred_element_type=jnp.float32)
    low_scores = (probs * (dprobs - delta_t[..., None])).astype(jnp.bfloat16)
    low_probs = probs.astype(jnp.bfloat16)
    query_term = jnp.einsum("tgij,tjd->tigd", low_scores, key_w, preferred_element_type=jnp.float32)
    key_w_term = jnp.einsum(
        "tgij,tigd->tjd", low_scores, query_t, preferred_element_type=jnp.float32
    )
    value_w_term = jnp.einsum(
        "tgij,tigd->tjd", low_probs, grad_t, preferred_element_type=jnp.float32
    )
    total = WINDOW_LENGTH + tokens
    key_term = jnp.zeros((total, depth), jnp.float32)
    value_term = jnp.zeros((total, depth), jnp.float32)
    for t in range(tiles):
        key_term = key_term.at[t * BLOCK : t * BLOCK + span].add(key_w_term[t])
        value_term = value_term.at[t * BLOCK : t * BLOCK + span].add(value_w_term[t])
    return (query_term.reshape(tokens, group, depth), key_term, value_term)


def on_device(
    queries, normed_keys, value_matrix, forward_out, output_gradient, row_log_total, pair_start
):
    grad_rows = lax.all_to_all(output_gradient, "head", split_axis=1, concat_axis=0, tiled=True)
    delta_rows = jnp.einsum(
        "thd,thd->ht", forward_out, grad_rows, preferred_element_type=jnp.float32
    )
    ring = lax.axis_size("sl")
    query_g = lax.all_to_all(queries, "sl", split_axis=1, concat_axis=0, tiled=True)
    grad_g = lax.all_to_all(grad_rows, "sl", split_axis=1, concat_axis=0, tiled=True)
    key_g = lax.all_to_all(normed_keys, "sl", split_axis=1, concat_axis=0, tiled=True)
    value_g = lax.all_to_all(value_matrix, "sl", split_axis=1, concat_axis=0, tiled=True)
    logsum_g = lax.all_to_all(row_log_total, "sl", split_axis=0, concat_axis=1, tiled=True)
    delta_g = lax.all_to_all(delta_rows, "sl", split_axis=0, concat_axis=1, tiled=True)
    start_g = lax.all_gather(pair_start, "sl", axis=0, tiled=True)
    tokens, group, depth = query_g.shape
    base = lax.axis_index("sh") * tokens
    key_own = key_g[:, 0]
    value_own = value_g[:, 0]
    key_far = shifted(key_own, "sh", 1)
    value_far = shifted(value_own, "sh", 1)
    keys = jnp.concatenate([key_far, key_own], axis=0)
    values = jnp.concatenate([value_far, value_own], axis=0)
    query_sum, key_sum, value_sum = band_terms(
        query_g, grad_g, logsum_g, delta_g, start_g, base, keys, values
    )
    key_back = shifted(key_sum[:WINDOW_LENGTH], "sh", -1)
    value_back = shifted(value_sum[:WINDOW_LENGTH], "sh", -1)
    key_total = key_sum[WINDOW_LENGTH:] + key_back
    value_total = value_sum[WINDOW_LENGTH:] + value_back
    query_grad = (query_sum * score_scale).astype(jnp.bfloat16)
    key_grad = (key_total * score_scale).astype(jnp.bfloat16)[:, None]
    value_grad = value_total.astype(jnp.bfloat16)[:, None]

    def back(x):
        x = lax.all_to_all(x, "sl", split_axis=0, concat_axis=1, tiled=True)
        return lax.all_to_all(x, "head", split_axis=0, concat_axis=1, tiled=True)

    return (back(query_grad), back(key_grad), back(value_grad))


def solution(mesh):
    head, seq = mesh.devices.shape
    ring = WINDOW_LENGTH // BLOCK
    grouped = Mesh(mesh.devices.reshape(head, seq // ring, ring), ("head", "sh", "sl"))
    seq_axes = ("sh", "sl")
    placed = (
        P(seq_axes, "head", None),
        P(seq_axes, "head", None),
        P(seq_axes, "head", None),
        P(seq_axes, "head", None),
        P(seq_axes + ("head",), None, None),
        P("head", seq_axes),
        P(seq_axes),
    )
    out = P(seq_axes + ("head",), None, None)
    return jax.shard_map(
        on_device, mesh=grouped, in_specs=placed, out_specs=(out, out, out), check_vma=False
    )
```

profile of v0, /device:TPU:4, one launch (start us, length us, event | category | flops | bytes accessed | tf_op | source)
XLA Modules:
  0.0 181.9 jit_solution(7914831301998009179)
XLA Ops:
  0.6 1.7 copy.58
  2.3 4.5 %all-to-all-start = ((bf16[256,4,128]{2,0,1:T(8,128)(2,1)}), bf16[256,4,128]{2,0,1:T(8,128)(2,1)S(1)}, u32[]{:S(2)}, u32[]{:S(2)}) async-start(bf16[256,4,128]{2,0,1:T(8,128)(2,1)} %copy.58), calls=%async_computation | async-start | bytes 524288 | tf_op jit(solution)/shard_map/all_to_all | solution.py:68
  6.9 10.4 %all-gather = s32[4,1,256]{2,1,0:T(1,128)S(1)} all-gather(s32[1,1,256]{2,1,0:T(1,128)} %bitcast.178), channel_id=1, replica_groups=mesh['head'=4,'sh'=32,'sl'=4] {'sl'}, dimensions={0}, use_global_device_ids=true | all-gather | bytes 5120 | tf_op jit(solution)/shard_map/all_gather | solution.py:72
  17.3 2.1 %copy.61 = bf16[64,32,128]{2,0,1:T(8,128)(2,1)} copy(bf16[64,32,128]{2,1,0:T(8,128)(2,1)} %param.27) | data formatting | bytes 1048576 | tf_op args[4]
  19.4 1.7 copy.60
  21.1 4.0 %all-to-all-start.3 = ((bf16[256,4,128]{2,0,1:T(8,128)(2,1)}), bf16[256,4,128]{2,0,1:T(8,128)(2,1)}, u32[]{:S(2)}, u32[]{:S(2)}) async-start(bf16[256,4,128]{2,0,1:T(8,128)(2,1)} %copy.60), calls=%async_computation.3 | async-start | bytes 524288 | tf_op jit(solution)/shard_map/all_to_all | solution.py:69
  25.2 6.7 %all-to-all-done.3 = bf16[256,4,128]{2,0,1:T(8,128)(2,1)} async-done(((bf16[256,4,128]{2,0,1:T(8,128)(2,1)}), bf16[256,4,128]{2,0,1:T(8,128)(2,1)}, u32[]{:S(2)}, u32[]{:S(2)}) %all-to-all-start.3) | async-done | bytes 262176 | tf_op jit(solution)/shard_map/all_to_all | solution.py:69
  31.8 3.5 %all-to-all-start.4 = ((bf16[64,32,128]{2,0,1:T(8,128)(2,1)}), bf16[64,32,128]{2,0,1:T(8,128)(2,1)S(1)}, u32[]{:S(2)}, u32[]{:S(2)}) async-start(bf16[64,32,128]{2,0,1:T(8,128)(2,1)} %copy.61), calls=%async_computation.4 | async-start | bytes 1048576 | tf_op jit(solution)/shard_map/all_to_all | solution.py:61
  35.3 1.9 %fusion.11 = pred[4,256,1280]{1,2,0:T(8,128)(4,1)S(1)} fusion(s32[4,256]{1,0:T(4,128)S(1)} %bitcast.177, s32[4,1280]{1,0:T(4,128)S(1)} %iota_add_fusion, s32[4,256]{1,0:T(4,128)S(1)} %iota_add_fusion.1), kind=kLoop, calls=%fused_computation.14 | loop fusion | flops 7864320 | bytes 1339392 | tf_op jit(solution)/shard_map/and | solution.py:33
  37.2 3.8 %collective-permute-start = (bf16[1024,128]{1,0:T(8,128)(2,1)S(1)}, bf16[1024,128]{1,0:T(8,128)(2,1)}, u32[]{:S(2)}, u32[]{:S(2)}) collective-permute-start(bf16[1024,128]{1,0:T(8,128)(2,1)S(1)} %bitcast.168), channel_id=1, source_target_pairs={{0,4},{4,8},{8,12},{12,16},{16,20},{20,24},{24,28},{28,32},{32,36}... | collective-permute-start | bytes 786440 | tf_op jit(solution)/shard_map/ppermute | solution.py:15
  41.0 1.1 bitcast_convert_fusion
  42.1 1.9 %copy.59 = bf16[256,8,128]{2,0,1:T(8,128)(2,1)} copy(bf16[256,8,128]{2,1,0:T(8,128)(2,1)} %param.23) | data formatting | bytes 1048576 | tf_op args[0]
  44.7 3.8 %collective-permute-start.1 = (bf16[1024,128]{1,0:T(8,128)(2,1)}, bf16[1024,128]{1,0:T(8,128)(2,1)}, u32[]{:S(2)}, u32[]{:S(2)}) collective-permute-start(bf16[1024,128]{1,0:T(8,128)(2,1)} %bitcast.18), channel_id=1, source_target_pairs={{0,4},{4,8},{8,12},{12,16},{16,20},{20,24},{24,28},{28,32},{32,36}... | collective-permute-start | bytes 786440 | tf_op jit(solution)/shard_map/ppermute | solution.py:15
  48.5 3.2 %all-to-all-start.2 = ((f32[4,2,256]{2,1,0:T(2,128)}), f32[4,2,256]{2,1,0:T(2,128)S(1)}, u32[]{:S(2)}, u32[]{:S(2)}) async-start(f32[4,2,256]{2,1,0:T(2,128)} %all_to_all.161), calls=%async_computation.2 | async-start | bytes 16384 | tf_op jit(solution)/shard_map/all_to_all | solution.py:70
  52.6 1.4 multiply_reduce_fusion
  54.6 2.4 %all-to-all-done.2 = f32[4,2,256]{2,1,0:T(2,128)S(1)} async-done(((f32[4,2,256]{2,1,0:T(2,128)}), f32[4,2,256]{2,1,0:T(2,128)S(1)}, u32[]{:S(2)}, u32[]{:S(2)}) %all-to-all-start.2) | async-done | bytes 8224 | tf_op jit(solution)/shard_map/all_to_all | solution.py:70
  57.0 3.5 %all-to-all-start.1 = ((bf16[256,8,128]{2,0,1:T(8,128)(2,1)}), bf16[256,8,128]{2,0,1:T(8,128)(2,1)S(1)}, u32[]{:S(2)}, u32[]{:S(2)}) async-start(bf16[256,8,128]{2,0,1:T(8,128)(2,1)} %copy.59), calls=%async_computation.1 | async-start | bytes 1048576 | tf_op jit(solution)/shard_map/all_to_all | solution.py:66
  60.5 1.3 fusion.47
  61.8 2.5 %fusion.41 = (bf16[1,1280,128]{2,1,0:T(8,128)(2,1)S(1)}, bf16[1,1280,128]{2,1,0:T(8,128)(2,1)}, bf16[1,1280,128]{2,1,0:T(8,128)(2,1)}, bf16[1,1280,128]{2,1,0:T(8,128)(2,1)}) fusion(bf16[1024,128]{1,0:T(8,128)(2,1)} %collective-permute-done.1, bf16[1024,128]{1,0:T(8,128)(2,1)} %bitcast.18), kind=kLoop, calls=%fused_computation.71 | loop fusion | flops 2621440 | bytes 1835008 | tf_op jit(solution)/shard_map/stack | solution.py:28
  64.4 5.2 %all-to-all-done.1 = bf16[256,8,128]{2,0,1:T(8,128)(2,1)S(1)} async-done(((bf16[256,8,128]{2,0,1:T(8,128)(2,1)}), bf16[256,8,128]{2,0,1:T(8,128)(2,1)S(1)}, u32[]{:S(2)}, u32[]{:S(2)}) %all-to-all-start.1) | async-done | bytes 524320 | tf_op jit(solution)/shard_map/all_to_all | solution.py:66
  69.5 4.1 %all-to-all-start.5 = ((bf16[256,8,128]{2,0,1:T(8,128)(2,1)}), bf16[256,8,128]{2,0,1:T(8,128)(2,1)}, u32[]{:S(2)}, u32[]{:S(2)}) async-start(bf16[256,8,128]{2,0,1:T(8,128)(2,1)} %bitcast.27), calls=%async_computation.5 | async-start | bytes 1048576 | tf_op jit(solution)/shard_map/all_to_all | solution.py:67
  73.7 5.5 %fusion.34 = f32[4,1280,256,2]{2,1,3,0:T(8,128)} fusion(bf16[4,256,2,128]{3,1,2,0:T(8,128)(2,1)S(1)} %bitcast.161, bf16[1,1280,128]{2,1,0:T(8,128)(2,1)S(1)} %get-tuple-element.105, bf16[1,1280,128]{2,1,0:T(8,128)(2,1)S(1)} %get-tuple-element.106, bf16[1,1280,128]{2,1,0:T(8,128)(2,1)S(1)} %get-tuple-element.104, ...), kind=kOutput, calls=%fused_computation.60 | convolution fusion | flops 676331520 | bytes 12320768 | tf_op jit(solution)/shard_map/tigd,tjd->tgij/dot_general | solution.py:35
  79.2 2.6 %all-to-all-done.5 = bf16[256,8,128]{2,0,1:T(8,128)(2,1)} async-done(((bf16[256,8,128]{2,0,1:T(8,128)(2,1)}), bf16[256,8,128]{2,0,1:T(8,128)(2,1)}, u32[]{:S(2)}, u32[]{:S(2)}) %all-to-all-start.5) | async-done | bytes 524320 | tf_op jit(solution)/shard_map/all_to_all | solution.py:67
  81.8 3.2 %all-to-all-start.6 = ((f32[4,2,256]{2,1,0:T(2,128)}), f32[4,2,256]{2,1,0:T(2,128)S(1)}, u32[]{:S(2)}, u32[]{:S(2)}) async-start(f32[4,2,256]{2,1,0:T(2,128)} %all_to_all.173), calls=%async_computation.6 | async-start | bytes 16384 | tf_op jit(solution)/shard_map/all_to_all | solution.py:71
  85.1 5.6 %fusion.13 = f32[4,1280,128]{2,1,0:T(8,128)S(1)} fusion(bf16[4,256,2,128]{3,1,2,0:T(8,128)(2,1)} %bitcast.29, f32[4,1280,256,2]{2,1,3,0:T(8,128)} %fusion.34, f32[4,2,256]{2,1,0:T(2,128)S(1)} %all-to-all-done.2, pred[4,256,1280]{1,2,0:T(8,128)(4,1)S(1)} %fusion.11), kind=kOutput, calls=%fused_computation.16 | convolution fusion | flops 681574400 | bytes 14950400 | tf_op jit(solution)/shard_map/tgij,tigd->tjd/dot_general | solution.py:46
  92.0 7.7 %collective-permute-start.3 = (f32[1024,128]{1,0:T(8,128)}, f32[1024,128]{1,0:T(8,128)}, u32[]{:S(2)}, u32[]{:S(2)}) collective-permute-start(f32[1024,128]{1,0:T(8,128)} %slice.261), channel_id=1, source_target_pairs={{4,0},{8,4},{12,8},{16,12},{20,16},{24,20},{28,24},{32,28},{36,32}... | collective-permute-start | bytes 1572872 | tf_op jit(solution)/shard_map/ppermute | solution.py:15
  99.8 6.2 %fusion.1 = bf16[4,2,256,1280]{2,3,1,0:T(8,128)(2,1)S(1)} fusion(f32[4,1280,256,2]{2,1,3,0:T(8,128)} %fusion.34, bf16[4,256,2,128]{3,1,2,0:T(8,128)(2,1)} %bitcast.29, f32[4,2,256]{2,1,0:T(2,128)S(1)} %all-to-all-done.6, f32[4,2,256]{2,1,0:T(2,128)S(1)} %all-to-all-done.2, pred[4,256,1280]{1,2,0:T(8,128)(4,1)S(1)} %fusion.11, ...), kind=kOutput, calls=%fused_computation.2 | convolution fusion | flops 692060160 | bytes 18890752 | tf_op jit(solution)/shard_map/tigd,tjd->tgij/dot_general | solution.py:39
  106.0 1.5 convolution_bitcast_fusion
  108.9 3.6 %collective-permute-start.2 = (f32[1024,128]{1,0:T(8,128)}, f32[1024,128]{1,0:T(8,128)}, u32[]{:S(2)}, u32[]{:S(2)}) collective-permute-start(f32[1024,128]{1,0:T(8,128)} %slice.253), channel_id=1, source_target_pairs={{4,0},{8,4},{12,8},{16,12},{20,16},{24,20},{28,24},{32,28},{36,32}... | collective-permute-start | bytes 1572872 | tf_op jit(solution)/shard_map/ppermute | solution.py:15
  112.6 1.7 fusion.23
  114.4 1.3 copy.65
  115.7 1.3 copy.66
  117.0 4.8 %all-to-all-start.7 = ((bf16[1024,2,128]{2,1,0:T(2,128)(2,1)}), bf16[1024,2,128]{2,1,0:T(2,128)(2,1)S(1)}, u32[]{:S(2)}, u32[]{:S(2)}) async-start(bf16[1024,2,128]{2,1,0:T(2,128)(2,1)} %copy.66), calls=%async_computation.7 | async-start | bytes 1048576 | tf_op jit(solution)/shard_map/all_to_all | solution.py:93
  121.8 1.1 fusion.53
  125.0 4.9 %all-to-all-done.7 = bf16[1024,2,128]{2,1,0:T(2,128)(2,1)S(1)} async-done(((bf16[1024,2,128]{2,1,0:T(2,128)(2,1)}), bf16[1024,2,128]{2,1,0:T(2,128)(2,1)S(1)}, u32[]{:S(2)}, u32[]{:S(2)}) %all-to-all-start.7) | async-done | bytes 524320 | tf_op jit(solution)/shard_map/all_to_all | solution.py:93
  129.8 3.4 %all-to-all-start.11 = ((bf16[4,2,16384]{2,1,0:T(2,128)(2,1)}), bf16[4,2,16384]{2,1,0:T(2,128)(2,1)S(1)}, u32[]{:S(2)}, u32[]{:S(2)}) async-start(bf16[4,2,16384]{2,1,0:T(2,128)(2,1)} %reshape.299), calls=%async_computation.11 | async-start | bytes 524288 | tf_op jit(solution)/shard_map/all_to_all | solution.py:93
  133.3 1.1 fusion.52
  136.0 3.9 %all-to-all-done.11 = bf16[4,2,16384]{2,1,0:T(2,128)(2,1)S(1)} async-done(((bf16[4,2,16384]{2,1,0:T(2,128)(2,1)}), bf16[4,2,16384]{2,1,0:T(2,128)(2,1)S(1)}, u32[]{:S(2)}, u32[]{:S(2)}) %all-to-all-start.11) | async-done | bytes 262176 | tf_op jit(solution)/shard_map/all_to_all | solution.py:93
  139.9 3.4 %all-to-all-start.9 = ((bf16[4,2,16384]{2,1,0:T(2,128)(2,1)}), bf16[4,2,16384]{2,1,0:T(2,128)(2,1)S(1)}, u32[]{:S(2)}, u32[]{:S(2)}) async-start(bf16[4,2,16384]{2,1,0:T(2,128)(2,1)} %reshape.297), calls=%async_computation.9 | async-start | bytes 524288 | tf_op jit(solution)/shard_map/all_to_all | solution.py:93
  143.4 1.1 copy.69
  144.6 5.4 %all-to-all-done.9 = bf16[4,2,16384]{2,1,0:T(2,128)(2,1)S(1)} async-done(((bf16[4,2,16384]{2,1,0:T(2,128)(2,1)}), bf16[4,2,16384]{2,1,0:T(2,128)(2,1)S(1)}, u32[]{:S(2)}, u32[]{:S(2)}) %all-to-all-start.9) | async-done | bytes 262176 | tf_op jit(solution)/shard_map/all_to_all | solution.py:93
  150.0 3.5 %all-to-all-start.8 = ((bf16[256,8,128]{2,1,0:T(8,128)(2,1)}), bf16[256,8,128]{2,1,0:T(8,128)(2,1)S(1)}, u32[]{:S(2)}, u32[]{:S(2)}) async-start(bf16[256,8,128]{2,1,0:T(8,128)(2,1)} %copy.69), calls=%async_computation.8 | async-start | bytes 1048576 | tf_op jit(solution)/shard_map/all_to_all | solution.py:94
  153.8 0.9 copy.75
  154.7 7.6 %all-to-all-done.8 = bf16[256,8,128]{2,1,0:T(8,128)(2,1)S(1)} async-done(((bf16[256,8,128]{2,1,0:T(8,128)(2,1)}), bf16[256,8,128]{2,1,0:T(8,128)(2,1)S(1)}, u32[]{:S(2)}, u32[]{:S(2)}) %all-to-all-start.8) | async-done | bytes 524320 | tf_op jit(solution)/shard_map/all_to_all | solution.py:94
  162.3 3.4 %all-to-all-start.12 = ((bf16[256,4,128]{2,1,0:T(4,128)(2,1)}), bf16[256,4,128]{2,1,0:T(4,128)(2,1)S(1)}, u32[]{:S(2)}, u32[]{:S(2)}) async-start(bf16[256,4,128]{2,1,0:T(4,128)(2,1)} %copy.75), calls=%async_computation.12 | async-start | bytes 524288 | tf_op jit(solution)/shard_map/all_to_all | solution.py:94
  166.9 4.7 %all-to-all-done.12 = bf16[256,4,128]{2,1,0:T(4,128)(2,1)S(1)} async-done(((bf16[256,4,128]{2,1,0:T(4,128)(2,1)}), bf16[256,4,128]{2,1,0:T(4,128)(2,1)S(1)}, u32[]{:S(2)}, u32[]{:S(2)}) %all-to-all-start.12) | async-done | bytes 262176 | tf_op jit(solution)/shard_map/all_to_all | solution.py:94
  171.7 3.4 %all-to-all-start.10 = ((bf16[256,4,128]{2,1,0:T(4,128)(2,1)}), bf16[256,4,128]{2,1,0:T(4,128)(2,1)S(1)}, u32[]{:S(2)}, u32[]{:S(2)}) async-start(bf16[256,4,128]{2,1,0:T(4,128)(2,1)} %copy.72), calls=%async_computation.10 | async-start | bytes 524288 | tf_op jit(solution)/shard_map/all_to_all | solution.py:94
  176.8 4.3 %all-to-all-done.10 = bf16[256,4,128]{2,1,0:T(4,128)(2,1)S(1)} async-done(((bf16[256,4,128]{2,1,0:T(4,128)(2,1)}), bf16[256,4,128]{2,1,0:T(4,128)(2,1)S(1)}, u32[]{:S(2)}, u32[]{:S(2)}) %all-to-all-start.10) | async-done | bytes 262176 | tf_op jit(solution)/shard_map/all_to_all | solution.py:94
  (57 shorter events, 12.8 us)
Async XLA Ops:
  2.3 18.7 %all-to-all-start = ((bf16[256,4,128]{2,0,1:T(8,128)(2,1)}), bf16[256,4,128]{2,0,1:T(8,128)(2,1)S(1)}, u32[]{:S(2)}, u32[]{:S(2)}) async-start(bf16[256,4,128]{2,0,1:T(8,128)(2,1)} %copy.58), calls=%async_computation | async-start | bytes 524288 | tf_op jit(solution)/shard_map/all_to_all | solution.py:68
  21.1 23.0 %copy-start.4 = (bf16[256,4,128]{2,0,1:T(8,128)(2,1)}, bf16[256,4,128]{2,0,1:T(8,128)(2,1)S(1)}, u32[]{:S(2)}) copy-start(bf16[256,4,128]{2,0,1:T(8,128)(2,1)S(1)} %all-to-all-done) | copy-start | bytes 786436
  21.1 10.8 %all-to-all-start.3 = ((bf16[256,4,128]{2,0,1:T(8,128)(2,1)}), bf16[256,4,128]{2,0,1:T(8,128)(2,1)}, u32[]{:S(2)}, u32[]{:S(2)}) async-start(bf16[256,4,128]{2,0,1:T(8,128)(2,1)} %copy.60), calls=%async_computation.3 | async-start | bytes 524288 | tf_op jit(solution)/shard_map/all_to_all | solution.py:69
  25.1 18.9 %copy-start.6 = (f32[8,256]{1,0:T(8,128)S(1)}, f32[8,256]{1,0:T(8,128)}, u32[]{:S(2)}) copy-start(f32[8,256]{1,0:T(8,128)} %param.28) | copy-start | bytes 24580
  31.8 16.6 %all-to-all-start.4 = ((bf16[64,32,128]{2,0,1:T(8,128)(2,1)}), bf16[64,32,128]{2,0,1:T(8,128)(2,1)S(1)}, u32[]{:S(2)}, u32[]{:S(2)}) async-start(bf16[64,32,128]{2,0,1:T(8,128)(2,1)} %copy.61), calls=%async_computation.4 | async-start | bytes 1048576 | tf_op jit(solution)/shard_map/all_to_all | solution.py:61
  37.2 23.3 %collective-permute-start = (bf16[1024,128]{1,0:T(8,128)(2,1)S(1)}, bf16[1024,128]{1,0:T(8,128)(2,1)}, u32[]{:S(2)}, u32[]{:S(2)}) collective-permute-start(bf16[1024,128]{1,0:T(8,128)(2,1)S(1)} %bitcast.168), channel_id=1, source_target_pairs={{0,4},{4,8},{8,12},{12,16},{16,20},{20,24},{24,28},{28,32},{32,36}... | collective-permute-start | bytes 786440 | tf_op jit(solution)/shard_map/ppermute | solution.py:15
  44.7 17.2 %collective-permute-start.1 = (bf16[1024,128]{1,0:T(8,128)(2,1)}, bf16[1024,128]{1,0:T(8,128)(2,1)}, u32[]{:S(2)}, u32[]{:S(2)}) collective-permute-start(bf16[1024,128]{1,0:T(8,128)(2,1)} %bitcast.18), channel_id=1, source_target_pairs={{0,4},{4,8},{8,12},{12,16},{16,20},{20,24},{24,28},{28,32},{32,36}... | collective-permute-start | bytes 786440 | tf_op jit(solution)/shard_map/ppermute | solution.py:15
  48.5 8.5 %all-to-all-start.2 = ((f32[4,2,256]{2,1,0:T(2,128)}), f32[4,2,256]{2,1,0:T(2,128)S(1)}, u32[]{:S(2)}, u32[]{:S(2)}) async-start(f32[4,2,256]{2,1,0:T(2,128)} %all_to_all.161), calls=%async_computation.2 | async-start | bytes 16384 | tf_op jit(solution)/shard_map/all_to_all | solution.py:70
  52.6 7.9 %copy-start.5 = (bf16[256,4,128]{2,0,1:T(8,128)(2,1)S(1)}, bf16[256,4,128]{2,0,1:T(8,128)(2,1)}, u32[]{:S(2)}) copy-start(bf16[256,4,128]{2,0,1:T(8,128)(2,1)} %copy-done.4) | copy-start | bytes 786436
  57.0 12.5 %all-to-all-start.1 = ((bf16[256,8,128]{2,0,1:T(8,128)(2,1)}), bf16[256,8,128]{2,0,1:T(8,128)(2,1)S(1)}, u32[]{:S(2)}, u32[]{:S(2)}) async-start(bf16[256,8,128]{2,0,1:T(8,128)(2,1)} %copy.59), calls=%async_computation.1 | async-start | bytes 1048576 | tf_op jit(solution)/shard_map/all_to_all | solution.py:66
  61.8 17.4 %copy-start = (bf16[1,1280,128]{2,1,0:T(8,128)(2,1)}, bf16[1,1280,128]{2,1,0:T(8,128)(2,1)S(1)}, u32[]{:S(2)}) copy-start(bf16[1,1280,128]{2,1,0:T(8,128)(2,1)S(1)} %get-tuple-element.105) | copy-start | bytes 983044
  61.8 17.4 %copy-start.2 = (bf16[1,1280,128]{2,1,0:T(8,128)(2,1)}, bf16[1,1280,128]{2,1,0:T(8,128)(2,1)S(1)}, u32[]{:S(2)}) copy-start(bf16[1,1280,128]{2,1,0:T(8,128)(2,1)S(1)} %get-tuple-element.106) | copy-start | bytes 983044
  69.5 12.3 %all-to-all-start.5 = ((bf16[256,8,128]{2,0,1:T(8,128)(2,1)}), bf16[256,8,128]{2,0,1:T(8,128)(2,1)}, u32[]{:S(2)}, u32[]{:S(2)}) async-start(bf16[256,8,128]{2,0,1:T(8,128)(2,1)} %bitcast.27), calls=%async_computation.5 | async-start | bytes 1048576 | tf_op jit(solution)/shard_map/all_to_all | solution.py:67
  81.8 17.9 %all-to-all-start.6 = ((f32[4,2,256]{2,1,0:T(2,128)}), f32[4,2,256]{2,1,0:T(2,128)S(1)}, u32[]{:S(2)}, u32[]{:S(2)}) async-start(f32[4,2,256]{2,1,0:T(2,128)} %all_to_all.173), calls=%async_computation.6 | async-start | bytes 16384 | tf_op jit(solution)/shard_map/all_to_all | solution.py:71
  92.0 29.7 %collective-permute-start.3 = (f32[1024,128]{1,0:T(8,128)}, f32[1024,128]{1,0:T(8,128)}, u32[]{:S(2)}, u32[]{:S(2)}) collective-permute-start(f32[1024,128]{1,0:T(8,128)} %slice.261), channel_id=1, source_target_pairs={{4,0},{8,4},{12,8},{16,12},{20,16},{24,20},{28,24},{32,28},{36,32}... | collective-permute-start | bytes 1572872 | tf_op jit(solution)/shard_map/ppermute | solution.py:15
  107.9 4.7 %copy-start.1 = (bf16[1,1280,128]{2,1,0:T(8,128)(2,1)S(1)}, bf16[1,1280,128]{2,1,0:T(8,128)(2,1)}, u32[]{:S(2)}) copy-start(bf16[1,1280,128]{2,1,0:T(8,128)(2,1)} %copy-done) | copy-start | bytes 983044
  107.9 4.7 %copy-start.3 = (bf16[1,1280,128]{2,1,0:T(8,128)(2,1)S(1)}, bf16[1,1280,128]{2,1,0:T(8,128)(2,1)}, u32[]{:S(2)}) copy-start(bf16[1,1280,128]{2,1,0:T(8,128)(2,1)} %copy-done.2) | copy-start | bytes 983044
  108.9 24.3 %collective-permute-start.2 = (f32[1024,128]{1,0:T(8,128)}, f32[1024,128]{1,0:T(8,128)}, u32[]{:S(2)}, u32[]{:S(2)}) collective-permute-start(f32[1024,128]{1,0:T(8,128)} %slice.253), channel_id=1, source_target_pairs={{4,0},{8,4},{12,8},{16,12},{20,16},{24,20},{28,24},{32,28},{36,32}... | collective-permute-start | bytes 1572872 | tf_op jit(solution)/shard_map/ppermute | solution.py:15
  117.0 12.8 %all-to-all-start.7 = ((bf16[1024,2,128]{2,1,0:T(2,128)(2,1)}), bf16[1024,2,128]{2,1,0:T(2,128)(2,1)S(1)}, u32[]{:S(2)}, u32[]{:S(2)}) async-start(bf16[1024,2,128]{2,1,0:T(2,128)(2,1)} %copy.66), calls=%async_computation.7 | async-start | bytes 1048576 | tf_op jit(solution)/shard_map/all_to_all | solution.py:93
  129.8 10.1 %all-to-all-start.11 = ((bf16[4,2,16384]{2,1,0:T(2,128)(2,1)}), bf16[4,2,16384]{2,1,0:T(2,128)(2,1)S(1)}, u32[]{:S(2)}, u32[]{:S(2)}) async-start(bf16[4,2,16384]{2,1,0:T(2,128)(2,1)} %reshape.299), calls=%async_computation.11 | async-start | bytes 524288 | tf_op jit(solution)/shard_map/all_to_all | solution.py:93
  139.9 10.1 %all-to-all-start.9 = ((bf16[4,2,16384]{2,1,0:T(2,128)(2,1)}), bf16[4,2,16384]{2,1,0:T(2,128)(2,1)S(1)}, u32[]{:S(2)}, u32[]{:S(2)}) async-start(bf16[4,2,16384]{2,1,0:T(2,128)(2,1)} %reshape.297), calls=%async_computation.9 | async-start | bytes 524288 | tf_op jit(solution)/shard_map/all_to_all | solution.py:93
  150.0 12.3 %all-to-all-start.8 = ((bf16[256,8,128]{2,1,0:T(8,128)(2,1)}), bf16[256,8,128]{2,1,0:T(8,128)(2,1)S(1)}, u32[]{:S(2)}, u32[]{:S(2)}) async-start(bf16[256,8,128]{2,1,0:T(8,128)(2,1)} %copy.69), calls=%async_computation.8 | async-start | bytes 1048576 | tf_op jit(solution)/shard_map/all_to_all | solution.py:94
  162.3 9.4 %all-to-all-start.12 = ((bf16[256,4,128]{2,1,0:T(4,128)(2,1)}), bf16[256,4,128]{2,1,0:T(4,128)(2,1)S(1)}, u32[]{:S(2)}, u32[]{:S(2)}) async-start(bf16[256,4,128]{2,1,0:T(4,128)(2,1)} %copy.75), calls=%async_computation.12 | async-start | bytes 524288 | tf_op jit(solution)/shard_map/all_to_all | solution.py:94
  171.7 9.4 %all-to-all-start.10 = ((bf16[256,4,128]{2,1,0:T(4,128)(2,1)}), bf16[256,4,128]{2,1,0:T(4,128)(2,1)S(1)}, u32[]{:S(2)}, u32[]{:S(2)}) async-start(bf16[256,4,128]{2,1,0:T(4,128)(2,1)} %copy.72), calls=%async_computation.10 | async-start | bytes 524288 | tf_op jit(solution)/shard_map/all_to_all | solution.py:94
where the time goes:
time: 183 us; the launch traced here: 182 us
  starting transfers between devices  66.9 us (37%)
  waiting for transfers between devices  47.6 us (26%)
  local copies, waits for them, and re-layouts  22.3 us (12%)
  matrix products  20.6 us (11%)
  other arithmetic  12.9 us (7%)
  blocking collectives  10.4 us (6%)
    ppermute x4, starting transfers between devices, shifted(): return lax.ppermute(value, axis, pairs)  19 us
    all_to_all x3, waiting for transfers between devices, back(): return lax.all_to_all(x, 'head', split_axis=0, concat_axis=1, tiled=True)  16.6 us
    all_to_all x3, waiting for transfers between devices, back(): x = lax.all_to_all(x, 'sl', split_axis=0, concat_axis=1, tiled=True)  14.2 us
    all_to_all x3, starting transfers between devices, back(): x = lax.all_to_all(x, 'sl', split_axis=0, concat_axis=1, tiled=True)  11.6 us
    all_gather x1, blocking collectives, on_device(): start_g = lax.all_gather(pair_start, 'sl', axis=0, tiled=True)  10.4 us
    all_to_all x3, starting transfers between devices, back(): return lax.all_to_all(x, 'head', split_axis=0, concat_axis=1, tiled=True)  10.3 us
    unnamed x25, local copies, waits for them, and re-layouts  9.52 us
    all_to_all x1, waiting for transfers between devices, on_device(): lax.all_to_all(value_matrix, 'sl', split_axis=1, concat_axis=0, tiled=True)  6.65 us
  transfers between devices with their start and end apart: 17, of which 10 were waited for; matrix products, arithmetic and copies ran while one was open for 29% of the time, Pallas kernels for 0%

commit v1 on v0

--- a/solution.py
+++ b/solution.py
@@ -66,7 +66,10 @@
     query_g = lax.all_to_all(queries, "sl", split_axis=1, concat_axis=0, tiled=True)
     grad_g = lax.all_to_all(grad_rows, "sl", split_axis=1, concat_axis=0, tiled=True)
     key_g = lax.all_to_all(normed_keys, "sl", split_axis=1, concat_axis=0, tiled=True)
-    value_g = lax.all_to_all(value_matrix, "sl", split_axis=1, concat_axis=0, tiled=True)
+    value_g = jnp.concatenate(
+        lax.all_to_all(jnp.stack(jnp.split(value_matrix, lax.axis_size("sl"), axis=1)), "sl", 0, 0),
+        axis=0,
+    )
     logsum_g = lax.all_to_all(row_log_total, "sl", split_axis=0, concat_axis=1, tiled=True)
     delta_g = lax.all_to_all(delta_rows, "sl", split_axis=0, concat_axis=1, tiled=True)
     start_g = lax.all_gather(pair_start, "sl", axis=0, tiled=True)

time: 183 us -> 183 us (level)
    unnamed x25 -> x28, local copies, waits for them, and re-layouts: 9.52 us -> 6.85 us
    split x0 -> x1, local copies, waits for them, and re-layouts: none -> 2.03 us  [on_device(): jnp.split(value_matrix, lax.axis_size('sl'), axis=1)]
where the time goes in v1:
time: 183 us; the launch traced here: 182 us
  starting transfers between devices  67.1 us (37%)
  waiting for transfers between devices  47.7 us (26%)
  local copies, waits for them, and re-layouts  21.7 us (12%)
  matrix products  20.6 us (11%)
  other arithmetic  13.6 us (7%)
  blocking collectives  10.2 us (6%)
    ppermute x4, starting transfers between devices, shifted(): return lax.ppermute(value, axis, pairs)  19.1 us
    all_to_all x3, waiting for transfers between devices, back(): return lax.all_to_all(x, 'head', split_axis=0, concat_axis=1, tiled=True)  16.6 us
    all_to_all x3, waiting for transfers between devices, back(): x = lax.all_to_all(x, 'sl', split_axis=0, concat_axis=1, tiled=True)  14.2 us
    all_to_all x3, starting transfers between devices, back(): x = lax.all_to_all(x, 'sl', split_axis=0, concat_axis=1, tiled=True)  11.5 us
    all_to_all x3, starting transfers between devices, back(): return lax.all_to_all(x, 'head', split_axis=0, concat_axis=1, tiled=True)  10.3 us
    all_gather x1, blocking collectives, on_device(): start_g = lax.all_gather(pair_start, 'sl', axis=0, tiled=True)  10.2 us
    unnamed x28, local copies, waits for them, and re-layouts  6.85 us
    all_to_all x1, waiting for transfers between devices, on_device(): lax.all_to_all(jnp.stack(jnp.split(value_matrix, lax.axis_size('sl'), axi...  6.65 us
  transfers between devices with their start and end apart: 17, of which 10 were waited for; matrix products, arithmetic and copies ran while one was open for 29% of the time, Pallas kernels for 0%

profile of v1, /device:TPU:4, one launch (start us, length us, event | category | flops | bytes accessed | tf_op | source)
XLA Modules:
  0.0 182.0 jit_solution(3846939707460195515)
XLA Ops:
  0.7 1.7 copy.69
  2.4 4.5 %all-to-all-start = ((bf16[256,4,128]{2,0,1:T(8,128)(2,1)}), bf16[256,4,128]{2,0,1:T(8,128)(2,1)S(1)}, u32[]{:S(2)}, u32[]{:S(2)}) async-start(bf16[256,4,128]{2,0,1:T(8,128)(2,1)} %copy.69), calls=%async_computation | async-start | bytes 524288 | tf_op jit(solution)/shard_map/all_to_all | solution.py:68
  6.9 2.0 %fusion.59 = (bf16[256,1,128]{2,1,0:T(2,128)(2,1)S(1)}, bf16[256,1,128]{2,1,0:T(2,128)(2,1)S(1)}, bf16[256,1,128]{2,1,0:T(2,128)(2,1)S(1)}, bf16[256,1,128]{2,1,0:T(2,128)(2,1)S(1)}) fusion(bf16[256,4,128]{2,1,0:T(4,128)(2,1)} %param.25), kind=kLoop, calls=%fused_computation.103 | loop fusion | bytes 524288 | tf_op jit(solution)/shard_map/split | solution.py:70
  9.0 10.2 %all-gather = s32[4,1,256]{2,1,0:T(1,128)S(1)} all-gather(s32[1,1,256]{2,1,0:T(1,128)S(1)} %bitcast.182), channel_id=1, replica_groups=mesh['head'=4,'sh'=32,'sl'=4] {'sl'}, dimensions={0}, use_global_device_ids=true | all-gather | bytes 5120 | tf_op jit(solution)/shard_map/all_gather | solution.py:75
  19.3 1.0 copy.75
  21.0 4.1 %all-to-all-start.3 = ((bf16[4,256,1,128]{3,1,2,0:T(8,128)(2,1)}), bf16[4,256,1,128]{3,1,2,0:T(8,128)(2,1)}, u32[]{:S(2)}, u32[]{:S(2)}) async-start(bf16[4,256,1,128]{3,1,2,0:T(8,128)(2,1)} %pad_maximum_fusion.2), calls=%async_computation.3 | async-start | bytes 524288 | tf_op jit(solution)/shard_map/all_to_all | solution.py:70
  25.1 6.7 %all-to-all-done.3 = bf16[4,256,1,128]{3,1,2,0:T(8,128)(2,1)} async-done(((bf16[4,256,1,128]{3,1,2,0:T(8,128)(2,1)}), bf16[4,256,1,128]{3,1,2,0:T(8,128)(2,1)}, u32[]{:S(2)}, u32[]{:S(2)}) %all-to-all-start.3) | async-done | bytes 262176 | tf_op jit(solution)/shard_map/all_to_all | solution.py:70
  31.8 3.5 %all-to-all-start.4 = ((bf16[64,32,128]{2,0,1:T(8,128)(2,1)}), bf16[64,32,128]{2,0,1:T(8,128)(2,1)S(1)}, u32[]{:S(2)}, u32[]{:S(2)}) async-start(bf16[64,32,128]{2,0,1:T(8,128)(2,1)} %copy.75), calls=%async_computation.4 | async-start | bytes 1048576 | tf_op jit(solution)/shard_map/all_to_all | solution.py:61
  35.3 1.9 %fusion.11 = pred[4,256,1280]{1,2,0:T(8,128)(4,1)S(1)} fusion(s32[4,256]{1,0:T(4,128)S(1)} %bitcast.181, s32[4,1280]{1,0:T(4,128)S(1)} %iota_add_fusion, s32[4,256]{1,0:T(4,128)S(1)} %iota_add_fusion.1), kind=kLoop, calls=%fused_computation.14 | loop fusion | flops 7864320 | bytes 1339392 | tf_op jit(solution)/shard_map/and | solution.py:33
  37.1 3.8 %collective-permute-start = (bf16[1024,128]{1,0:T(8,128)(2,1)S(1)}, bf16[1024,128]{1,0:T(8,128)(2,1)}, u32[]{:S(2)}, u32[]{:S(2)}) collective-permute-start(bf16[1024,128]{1,0:T(8,128)(2,1)S(1)} %bitcast.172), channel_id=1, source_target_pairs={{0,4},{4,8},{8,12},{12,16},{16,20},{20,24},{24,28},{28,32},{32,36}... | collective-permute-start | bytes 786440 | tf_op jit(solution)/shard_map/ppermute | solution.py:15
  41.0 1.1 bitcast_convert_fusion
  42.1 1.9 %copy.70 = bf16[256,8,128]{2,0,1:T(8,128)(2,1)} copy(bf16[256,8,128]{2,1,0:T(8,128)(2,1)} %param.23) | data formatting | bytes 1048576 | tf_op args[0]
  44.6 3.8 %collective-permute-start.1 = (bf16[1024,128]{1,0:T(8,128)(2,1)}, bf16[1024,128]{1,0:T(8,128)(2,1)}, u32[]{:S(2)}, u32[]{:S(2)}) collective-permute-start(bf16[1024,128]{1,0:T(8,128)(2,1)} %bitcast.20), channel_id=1, source_target_pairs={{0,4},{4,8},{8,12},{12,16},{16,20},{20,24},{24,28},{28,32},{32,36}... | collective-permute-start | bytes 786440 | tf_op jit(solution)/shard_map/ppermute | solution.py:15
  48.4 3.2 %all-to-all-start.2 = ((f32[4,2,256]{2,1,0:T(2,128)}), f32[4,2,256]{2,1,0:T(2,128)S(1)}, u32[]{:S(2)}, u32[]{:S(2)}) async-start(f32[4,2,256]{2,1,0:T(2,128)} %all_to_all.153), calls=%async_computation.2 | async-start | bytes 16384 | tf_op jit(solution)/shard_map/all_to_all | solution.py:73
  52.6 1.4 multiply_reduce_fusion
  54.6 2.4 %all-to-all-done.2 = f32[4,2,256]{2,1,0:T(2,128)S(1)} async-done(((f32[4,2,256]{2,1,0:T(2,128)}), f32[4,2,256]{2,1,0:T(2,128)S(1)}, u32[]{:S(2)}, u32[]{:S(2)}) %all-to-all-start.2) | async-done | bytes 8224 | tf_op jit(solution)/shard_map/all_to_all | solution.py:73
  57.0 3.5 %all-to-all-start.1 = ((bf16[256,8,128]{2,0,1:T(8,128)(2,1)}), bf16[256,8,128]{2,0,1:T(8,128)(2,1)S(1)}, u32[]{:S(2)}, u32[]{:S(2)}) async-start(bf16[256,8,128]{2,0,1:T(8,128)(2,1)} %copy.70), calls=%async_computation.1 | async-start | bytes 1048576 | tf_op jit(solution)/shard_map/all_to_all | solution.py:66
  60.5 1.3 fusion.47
  61.8 2.5 %fusion.41 = (bf16[1,1280,128]{2,1,0:T(8,128)(2,1)S(1)}, bf16[1,1280,128]{2,1,0:T(8,128)(2,1)}, bf16[1,1280,128]{2,1,0:T(8,128)(2,1)}, bf16[1,1280,128]{2,1,0:T(8,128)(2,1)}) fusion(bf16[1024,128]{1,0:T(8,128)(2,1)} %collective-permute-done.1, bf16[1024,128]{1,0:T(8,128)(2,1)} %bitcast.20), kind=kLoop, calls=%fused_computation.71 | loop fusion | flops 2621440 | bytes 1835008 | tf_op jit(solution)/shard_map/stack | solution.py:28
  64.3 5.2 %all-to-all-done.1 = bf16[256,8,128]{2,0,1:T(8,128)(2,1)S(1)} async-done(((bf16[256,8,128]{2,0,1:T(8,128)(2,1)}), bf16[256,8,128]{2,0,1:T(8,128)(2,1)S(1)}, u32[]{:S(2)}, u32[]{:S(2)}) %all-to-all-start.1) | async-done | bytes 524320 | tf_op jit(solution)/shard_map/all_to_all | solution.py:66
  69.5 4.1 %all-to-all-start.5 = ((bf16[256,8,128]{2,0,1:T(8,128)(2,1)}), bf16[256,8,128]{2,0,1:T(8,128)(2,1)}, u32[]{:S(2)}, u32[]{:S(2)}) async-start(bf16[256,8,128]{2,0,1:T(8,128)(2,1)} %bitcast.29), calls=%async_computation.5 | async-start | bytes 1048576 | tf_op jit(solution)/shard_map/all_to_all | solution.py:67
  73.6 5.6 %fusion.34 = f32[4,1280,256,2]{2,1,3,0:T(8,128)} fusion(bf16[4,256,2,128]{3,1,2,0:T(8,128)(2,1)S(1)} %bitcast.165, bf16[1,1280,128]{2,1,0:T(8,128)(2,1)S(1)} %get-tuple-element.105, bf16[1,1280,128]{2,1,0:T(8,128)(2,1)S(1)} %get-tuple-element.106, bf16[1,1280,128]{2,1,0:T(8,128)(2,1)S(1)} %get-tuple-element.104, ...), kind=kOutput, calls=%fused_computation.60 | convolution fusion | flops 676331520 | bytes 12320768 | tf_op jit(solution)/shard_map/tigd,tjd->tgij/dot_general | solution.py:35
  79.2 2.6 %all-to-all-done.5 = bf16[256,8,128]{2,0,1:T(8,128)(2,1)} async-done(((bf16[256,8,128]{2,0,1:T(8,128)(2,1)}), bf16[256,8,128]{2,0,1:T(8,128)(2,1)}, u32[]{:S(2)}, u32[]{:S(2)}) %all-to-all-start.5) | async-done | bytes 524320 | tf_op jit(solution)/shard_map/all_to_all | solution.py:67
  81.8 3.2 %all-to-all-start.6 = ((f32[4,2,256]{2,1,0:T(2,128)}), f32[4,2,256]{2,1,0:T(2,128)S(1)}, u32[]{:S(2)}, u32[]{:S(2)}) async-start(f32[4,2,256]{2,1,0:T(2,128)} %all_to_all.163), calls=%async_computation.6 | async-start | bytes 16384 | tf_op jit(solution)/shard_map/all_to_all | solution.py:74
  85.0 5.6 %fusion.13 = f32[4,1280,128]{2,1,0:T(8,128)S(1)} fusion(bf16[4,256,2,128]{3,1,2,0:T(8,128)(2,1)} %bitcast.31, f32[4,1280,256,2]{2,1,3,0:T(8,128)} %fusion.34, f32[4,2,256]{2,1,0:T(2,128)S(1)} %all-to-all-done.2, pred[4,256,1280]{1,2,0:T(8,128)(4,1)S(1)} %fusion.11), kind=kOutput, calls=%fused_computation.16 | convolution fusion | flops 681574400 | bytes 14950400 | tf_op jit(solution)/shard_map/tgij,tigd->tjd/dot_general | solution.py:46
  92.0 7.7 %collective-permute-start.3 = (f32[1024,128]{1,0:T(8,128)}, f32[1024,128]{1,0:T(8,128)}, u32[]{:S(2)}, u32[]{:S(2)}) collective-permute-start(f32[1024,128]{1,0:T(8,128)} %slice.261), channel_id=1, source_target_pairs={{4,0},{8,4},{12,8},{16,12},{20,16},{24,20},{28,24},{32,28},{36,32}... | collective-permute-start | bytes 1572872 | tf_op jit(solution)/shard_map/ppermute | solution.py:15
  99.7 6.2 %fusion.1 = bf16[4,2,256,1280]{2,3,1,0:T(8,128)(2,1)S(1)} fusion(f32[4,1280,256,2]{2,1,3,0:T(8,128)} %fusion.34, bf16[4,256,2,128]{3,1,2,0:T(8,128)(2,1)} %bitcast.31, f32[4,2,256]{2,1,0:T(2,128)S(1)} %all-to-all-done.6, f32[4,2,256]{2,1,0:T(2,128)S(1)} %all-to-all-done.2, pred[4,256,1280]{1,2,0:T(8,128)(4,1)S(1)} %fusion.11, ...), kind=kOutput, calls=%fused_computation.2 | convolution fusion | flops 692060160 | bytes 18890752 | tf_op jit(solution)/shard_map/tigd,tjd->tgij/dot_general | solution.py:39
  105.9 1.5 convolution_bitcast_fusion
  108.9 3.8 %collective-permute-start.2 = (f32[1024,128]{1,0:T(8,128)}, f32[1024,128]{1,0:T(8,128)}, u32[]{:S(2)}, u32[]{:S(2)}) collective-permute-start(f32[1024,128]{1,0:T(8,128)} %slice.253), channel_id=1, source_target_pairs={{4,0},{8,4},{12,8},{16,12},{20,16},{24,20},{28,24},{32,28},{36,32}... | collective-permute-start | bytes 1572872 | tf_op jit(solution)/shard_map/ppermute | solution.py:15
  112.7 1.8 fusion.23
  114.5 1.3 copy.79
  115.8 1.3 copy.80
  117.2 4.7 %all-to-all-start.7 = ((bf16[1024,2,128]{2,1,0:T(2,128)(2,1)}), bf16[1024,2,128]{2,1,0:T(2,128)(2,1)S(1)}, u32[]{:S(2)}, u32[]{:S(2)}) async-start(bf16[1024,2,128]{2,1,0:T(2,128)(2,1)} %copy.80), calls=%async_computation.7 | async-start | bytes 1048576 | tf_op jit(solution)/shard_map/all_to_all | solution.py:96
  121.9 1.1 fusion.53
  125.1 4.9 %all-to-all-done.7 = bf16[1024,2,128]{2,1,0:T(2,128)(2,1)S(1)} async-done(((bf16[1024,2,128]{2,1,0:T(2,128)(2,1)}), bf16[1024,2,128]{2,1,0:T(2,128)(2,1)S(1)}, u32[]{:S(2)}, u32[]{:S(2)}) %all-to-all-start.7) | async-done | bytes 524320 | tf_op jit(solution)/shard_map/all_to_all | solution.py:96
  130.0 3.4 %all-to-all-start.11 = ((bf16[4,2,16384]{2,1,0:T(2,128)(2,1)}), bf16[4,2,16384]{2,1,0:T(2,128)(2,1)S(1)}, u32[]{:S(2)}, u32[]{:S(2)}) async-start(bf16[4,2,16384]{2,1,0:T(2,128)(2,1)} %reshape.298), calls=%async_computation.11 | async-start | bytes 524288 | tf_op jit(solution)/shard_map/all_to_all | solution.py:96
  133.4 1.1 fusion.52
  136.1 3.9 %all-to-all-done.11 = bf16[4,2,16384]{2,1,0:T(2,128)(2,1)S(1)} async-done(((bf16[4,2,16384]{2,1,0:T(2,128)(2,1)}), bf16[4,2,16384]{2,1,0:T(2,128)(2,1)S(1)}, u32[]{:S(2)}, u32[]{:S(2)}) %all-to-all-start.11) | async-done | bytes 262176 | tf_op jit(solution)/shard_map/all_to_all | solution.py:96
  140.0 3.4 %all-to-all-start.9 = ((bf16[4,2,16384]{2,1,0:T(2,128)(2,1)}), bf16[4,2,16384]{2,1,0:T(2,128)(2,1)S(1)}, u32[]{:S(2)}, u32[]{:S(2)}) async-start(bf16[4,2,16384]{2,1,0:T(2,128)(2,1)} %reshape.296), calls=%async_computation.9 | async-start | bytes 524288 | tf_op jit(solution)/shard_map/all_to_all | solution.py:96
  143.6 1.1 copy.83
  144.7 5.4 %all-to-all-done.9 = bf16[4,2,16384]{2,1,0:T(2,128)(2,1)S(1)} async-done(((bf16[4,2,16384]{2,1,0:T(2,128)(2,1)}), bf16[4,2,16384]{2,1,0:T(2,128)(2,1)S(1)}, u32[]{:S(2)}, u32[]{:S(2)}) %all-to-all-start.9) | async-done | bytes 262176 | tf_op jit(solution)/shard_map/all_to_all | solution.py:96
  150.1 3.5 %all-to-all-start.8 = ((bf16[256,8,128]{2,1,0:T(8,128)(2,1)}), bf16[256,8,128]{2,1,0:T(8,128)(2,1)S(1)}, u32[]{:S(2)}, u32[]{:S(2)}) async-start(bf16[256,8,128]{2,1,0:T(8,128)(2,1)} %copy.83), calls=%async_computation.8 | async-start | bytes 1048576 | tf_op jit(solution)/shard_map/all_to_all | solution.py:97
  153.9 0.9 copy.89
  154.8 7.6 %all-to-all-done.8 = bf16[256,8,128]{2,1,0:T(8,128)(2,1)S(1)} async-done(((bf16[256,8,128]{2,1,0:T(8,128)(2,1)}), bf16[256,8,128]{2,1,0:T(8,128)(2,1)S(1)}, u32[]{:S(2)}, u32[]{:S(2)}) %all-to-all-start.8) | async-done | bytes 524320 | tf_op jit(solution)/shard_map/all_to_all | solution.py:97
  162.4 3.4 %all-to-all-start.12 = ((bf16[256,4,128]{2,1,0:T(4,128)(2,1)}), bf16[256,4,128]{2,1,0:T(4,128)(2,1)S(1)}, u32[]{:S(2)}, u32[]{:S(2)}) async-start(bf16[256,4,128]{2,1,0:T(4,128)(2,1)} %copy.89), calls=%async_computation.12 | async-start | bytes 524288 | tf_op jit(solution)/shard_map/all_to_all | solution.py:97
  167.1 4.7 %all-to-all-done.12 = bf16[256,4,128]{2,1,0:T(4,128)(2,1)S(1)} async-done(((bf16[256,4,128]{2,1,0:T(4,128)(2,1)}), bf16[256,4,128]{2,1,0:T(4,128)(2,1)S(1)}, u32[]{:S(2)}, u32[]{:S(2)}) %all-to-all-start.12) | async-done | bytes 262176 | tf_op jit(solution)/shard_map/all_to_all | solution.py:97
  171.8 3.4 %all-to-all-start.10 = ((bf16[256,4,128]{2,1,0:T(4,128)(2,1)}), bf16[256,4,128]{2,1,0:T(4,128)(2,1)S(1)}, u32[]{:S(2)}, u32[]{:S(2)}) async-start(bf16[256,4,128]{2,1,0:T(4,128)(2,1)} %copy.86), calls=%async_computation.10 | async-start | bytes 524288 | tf_op jit(solution)/shard_map/all_to_all | solution.py:97
  176.9 4.3 %all-to-all-done.10 = bf16[256,4,128]{2,1,0:T(4,128)(2,1)S(1)} async-done(((bf16[256,4,128]{2,1,0:T(4,128)(2,1)}), bf16[256,4,128]{2,1,0:T(4,128)(2,1)S(1)}, u32[]{:S(2)}, u32[]{:S(2)}) %all-to-all-start.10) | async-done | bytes 262176 | tf_op jit(solution)/shard_map/all_to_all | solution.py:97
  (64 shorter events, 13.6 us)
Async XLA Ops:
  0.6 8.4 %copy-start.8 = (s32[256]{0:T(256)S(1)}, s32[256]{0:T(256)}, u32[]{:S(2)}) copy-start(s32[256]{0:T(256)} %param.29) | copy-start | bytes 3076
  0.6 18.6 %copy-start.6 = (bf16[64,32,128]{2,1,0:T(8,128)(2,1)S(1)}, bf16[64,32,128]{2,1,0:T(8,128)(2,1)}, u32[]{:S(2)}) copy-start(bf16[64,32,128]{2,1,0:T(8,128)(2,1)} %param.27) | copy-start | bytes 1572868
  2.4 18.6 %all-to-all-start = ((bf16[256,4,128]{2,0,1:T(8,128)(2,1)}), bf16[256,4,128]{2,0,1:T(8,128)(2,1)S(1)}, u32[]{:S(2)}, u32[]{:S(2)}) async-start(bf16[256,4,128]{2,0,1:T(8,128)(2,1)} %copy.69), calls=%async_computation | async-start | bytes 524288 | tf_op jit(solution)/shard_map/all_to_all | solution.py:68
  21.0 23.0 %copy-start.4 = (bf16[256,4,128]{2,0,1:T(8,128)(2,1)}, bf16[256,4,128]{2,0,1:T(8,128)(2,1)S(1)}, u32[]{:S(2)}) copy-start(bf16[256,4,128]{2,0,1:T(8,128)(2,1)S(1)} %all-to-all-done) | copy-start | bytes 786436
  21.0 10.8 %all-to-all-start.3 = ((bf16[4,256,1,128]{3,1,2,0:T(8,128)(2,1)}), bf16[4,256,1,128]{3,1,2,0:T(8,128)(2,1)}, u32[]{:S(2)}, u32[]{:S(2)}) async-start(bf16[4,256,1,128]{3,1,2,0:T(8,128)(2,1)} %pad_maximum_fusion.2), calls=%async_computation.3 | async-start | bytes 524288 | tf_op jit(solution)/shard_map/all_to_all | solution.py:70
  25.1 18.9 %copy-start.7 = (f32[8,256]{1,0:T(8,128)S(1)}, f32[8,256]{1,0:T(8,128)}, u32[]{:S(2)}) copy-start(f32[8,256]{1,0:T(8,128)} %param.28) | copy-start | bytes 24580
  31.8 16.6 %all-to-all-start.4 = ((bf16[64,32,128]{2,0,1:T(8,128)(2,1)}), bf16[64,32,128]{2,0,1:T(8,128)(2,1)S(1)}, u32[]{:S(2)}, u32[]{:S(2)}) async-start(bf16[64,32,128]{2,0,1:T(8,128)(2,1)} %copy.75), calls=%async_computation.4 | async-start | bytes 1048576 | tf_op jit(solution)/shard_map/all_to_all | solution.py:61
  37.1 23.3 %collective-permute-start = (bf16[1024,128]{1,0:T(8,128)(2,1)S(1)}, bf16[1024,128]{1,0:T(8,128)(2,1)}, u32[]{:S(2)}, u32[]{:S(2)}) collective-permute-start(bf16[1024,128]{1,0:T(8,128)(2,1)S(1)} %bitcast.172), channel_id=1, source_target_pairs={{0,4},{4,8},{8,12},{12,16},{16,20},{20,24},{24,28},{28,32},{32,36}... | collective-permute-start | bytes 786440 | tf_op jit(solution)/shard_map/ppermute | solution.py:15
  44.6 17.2 %collective-permute-start.1 = (bf16[1024,128]{1,0:T(8,128)(2,1)}, bf16[1024,128]{1,0:T(8,128)(2,1)}, u32[]{:S(2)}, u32[]{:S(2)}) collective-permute-start(bf16[1024,128]{1,0:T(8,128)(2,1)} %bitcast.20), channel_id=1, source_target_pairs={{0,4},{4,8},{8,12},{12,16},{16,20},{20,24},{24,28},{28,32},{32,36}... | collective-permute-start | bytes 786440 | tf_op jit(solution)/shard_map/ppermute | solution.py:15
  48.4 8.5 %all-to-all-start.2 = ((f32[4,2,256]{2,1,0:T(2,128)}), f32[4,2,256]{2,1,0:T(2,128)S(1)}, u32[]{:S(2)}, u32[]{:S(2)}) async-start(f32[4,2,256]{2,1,0:T(2,128)} %all_to_all.153), calls=%async_computation.2 | async-start | bytes 16384 | tf_op jit(solution)/shard_map/all_to_all | solution.py:73
  52.6 7.9 %copy-start.5 = (bf16[256,4,128]{2,0,1:T(8,128)(2,1)S(1)}, bf16[256,4,128]{2,0,1:T(8,128)(2,1)}, u32[]{:S(2)}) copy-start(bf16[256,4,128]{2,0,1:T(8,128)(2,1)} %copy-done.4) | copy-start | bytes 786436
  57.0 12.5 %all-to-all-start.1 = ((bf16[256,8,128]{2,0,1:T(8,128)(2,1)}), bf16[256,8,128]{2,0,1:T(8,128)(2,1)S(1)}, u32[]{:S(2)}, u32[]{:S(2)}) async-start(bf16[256,8,128]{2,0,1:T(8,128)(2,1)} %copy.70), calls=%async_computation.1 | async-start | bytes 1048576 | tf_op jit(solution)/shard_map/all_to_all | solution.py:66
  61.8 17.4 %copy-start = (bf16[1,1280,128]{2,1,0:T(8,128)(2,1)}, bf16[1,1280,128]{2,1,0:T(8,128)(2,1)S(1)}, u32[]{:S(2)}) copy-start(bf16[1,1280,128]{2,1,0:T(8,128)(2,1)S(1)} %get-tuple-element.105) | copy-start | bytes 983044
  61.8 17.4 %copy-start.2 = (bf16[1,1280,128]{2,1,0:T(8,128)(2,1)}, bf16[1,1280,128]{2,1,0:T(8,128)(2,1)S(1)}, u32[]{:S(2)}) copy-start(bf16[1,1280,128]{2,1,0:T(8,128)(2,1)S(1)} %get-tuple-element.106) | copy-start | bytes 983044
  69.5 12.3 %all-to-all-start.5 = ((bf16[256,8,128]{2,0,1:T(8,128)(2,1)}), bf16[256,8,128]{2,0,1:T(8,128)(2,1)}, u32[]{:S(2)}, u32[]{:S(2)}) async-start(bf16[256,8,128]{2,0,1:T(8,128)(2,1)} %bitcast.29), calls=%async_computation.5 | async-start | bytes 1048576 | tf_op jit(solution)/shard_map/all_to_all | solution.py:67
  81.8 17.9 %all-to-all-start.6 = ((f32[4,2,256]{2,1,0:T(2,128)}), f32[4,2,256]{2,1,0:T(2,128)S(1)}, u32[]{:S(2)}, u32[]{:S(2)}) async-start(f32[4,2,256]{2,1,0:T(2,128)} %all_to_all.163), calls=%async_computation.6 | async-start | bytes 16384 | tf_op jit(solution)/shard_map/all_to_all | solution.py:74
  92.0 29.9 %collective-permute-start.3 = (f32[1024,128]{1,0:T(8,128)}, f32[1024,128]{1,0:T(8,128)}, u32[]{:S(2)}, u32[]{:S(2)}) collective-permute-start(f32[1024,128]{1,0:T(8,128)} %slice.261), channel_id=1, source_target_pairs={{4,0},{8,4},{12,8},{16,12},{20,16},{24,20},{28,24},{32,28},{36,32}... | collective-permute-start | bytes 1572872 | tf_op jit(solution)/shard_map/ppermute | solution.py:15
  107.9 4.8 %copy-start.1 = (bf16[1,1280,128]{2,1,0:T(8,128)(2,1)S(1)}, bf16[1,1280,128]{2,1,0:T(8,128)(2,1)}, u32[]{:S(2)}) copy-start(bf16[1,1280,128]{2,1,0:T(8,128)(2,1)} %copy-done) | copy-start | bytes 983044
  107.9 4.8 %copy-start.3 = (bf16[1,1280,128]{2,1,0:T(8,128)(2,1)S(1)}, bf16[1,1280,128]{2,1,0:T(8,128)(2,1)}, u32[]{:S(2)}) copy-start(bf16[1,1280,128]{2,1,0:T(8,128)(2,1)} %copy-done.2) | copy-start | bytes 983044
  108.9 24.5 %collective-permute-start.2 = (f32[1024,128]{1,0:T(8,128)}, f32[1024,128]{1,0:T(8,128)}, u32[]{:S(2)}, u32[]{:S(2)}) collective-permute-start(f32[1024,128]{1,0:T(8,128)} %slice.253), channel_id=1, source_target_pairs={{4,0},{8,4},{12,8},{16,12},{20,16},{24,20},{28,24},{32,28},{36,32}... | collective-permute-start | bytes 1572872 | tf_op jit(solution)/shard_map/ppermute | solution.py:15
  117.2 12.8 %all-to-all-start.7 = ((bf16[1024,2,128]{2,1,0:T(2,128)(2,1)}), bf16[1024,2,128]{2,1,0:T(2,128)(2,1)S(1)}, u32[]{:S(2)}, u32[]{:S(2)}) async-start(bf16[1024,2,128]{2,1,0:T(2,128)(2,1)} %copy.80), calls=%async_computation.7 | async-start | bytes 1048576 | tf_op jit(solution)/shard_map/all_to_all | solution.py:96
  130.0 10.1 %all-to-all-start.11 = ((bf16[4,2,16384]{2,1,0:T(2,128)(2,1)}), bf16[4,2,16384]{2,1,0:T(2,128)(2,1)S(1)}, u32[]{:S(2)}, u32[]{:S(2)}) async-start(bf16[4,2,16384]{2,1,0:T(2,128)(2,1)} %reshape.298), calls=%async_computation.11 | async-start | bytes 524288 | tf_op jit(solution)/shard_map/all_to_all | solution.py:96
  140.0 10.1 %all-to-all-start.9 = ((bf16[4,2,16384]{2,1,0:T(2,128)(2,1)}), bf16[4,2,16384]{2,1,0:T(2,128)(2,1)S(1)}, u32[]{:S(2)}, u32[]{:S(2)}) async-start(bf16[4,2,16384]{2,1,0:T(2,128)(2,1)} %reshape.296), calls=%async_computation.9 | async-start | bytes 524288 | tf_op jit(solution)/shard_map/all_to_all | solution.py:96
  150.1 12.3 %all-to-all-start.8 = ((bf16[256,8,128]{2,1,0:T(8,128)(2,1)}), bf16[256,8,128]{2,1,0:T(8,128)(2,1)S(1)}, u32[]{:S(2)}, u32[]{:S(2)}) async-start(bf16[256,8,128]{2,1,0:T(8,128)(2,1)} %copy.83), calls=%async_computation.8 | async-start | bytes 1048576 | tf_op jit(solution)/shard_map/all_to_all | solution.py:97
  162.4 9.4 %all-to-all-start.12 = ((bf16[256,4,128]{2,1,0:T(4,128)(2,1)}), bf16[256,4,128]{2,1,0:T(4,128)(2,1)S(1)}, u32[]{:S(2)}, u32[]{:S(2)}) async-start(bf16[256,4,128]{2,1,0:T(4,128)(2,1)} %copy.89), calls=%async_computation.12 | async-start | bytes 524288 | tf_op jit(solution)/shard_map/all_to_all | solution.py:97
  171.8 9.4 %all-to-all-start.10 = ((bf16[256,4,128]{2,1,0:T(4,128)(2,1)}), bf16[256,4,128]{2,1,0:T(4,128)(2,1)S(1)}, u32[]{:S(2)}, u32[]{:S(2)}) async-start(bf16[256,4,128]{2,1,0:T(4,128)(2,1)} %copy.86), calls=%async_computation.10 | async-start | bytes 524288 | tf_op jit(solution)/shard_map/all_to_all | solution.py:97
